TPU v7x, 32 devices: a whole 2x2x4 slice. The times are simulated.
32 devices in a mesh: req: 16 (over z, x, core), ep: 2 (over y).
Axes of the slice: x: 2, y: 2, z: 4, core: 2. Of those that a mesh axis runs over, the one named last changes fastest.
Arguments:
- hidden: bfloat16 [16, 512, 1536], P('req', None, 'ep'), may hold values from -6 to 6
- key_cache: bfloat16 [16, 8, 2560, 64], P('req', 'ep'), may hold values from -160 to 160
- value_cache: bfloat16 [16, 8, 2560, 64], P('req', 'ep'), may hold values from -6 to 6
- request_order: int32 [16], replicated, may hold values from 0 to 15, each once
- cached_lengths: int32 [16], replicated, may hold values from 1 to 2048, 16384 in all
- expert_ids: int32 [16, 512, 8], P('req'), may hold values from 0 to 39, all different within a row; in each aligned block of 512 rows (0 to 511, 512 to 1023, ..., all dimensions but the last counted through in order) at most 192 rows name the same one
- gate_values: float32 [16, 512, 8], P('req'), may hold values from 0.1 to 1
- attn_gain: float32 [1536], replicated, may hold values from 0.25 to 1.75
- ffn_gain: float32 [1536], replicated, may hold values from 0.25 to 1.75
- w_query: bfloat16 [1536, 1536], P(None, 'ep'), may hold values from -0.15625 to 0.15625
- w_key: bfloat16 [1536, 512], P(None, 'ep'), may hold values from -0.15625 to 0.15625
- w_value: bfloat16 [1536, 512], P(None, 'ep'), may hold values from -0.15625 to 0.15625
- w_out: bfloat16 [1536, 1536], P('ep'), may hold values from -0.15625 to 0.15625
- expert_gate: bfloat16 [4, 1536, 512], P('ep', 'req'), may hold values from -0.15625 to 0.15625
- expert_up: bfloat16 [4, 1536, 512], P('ep', 'req'), may hold values from -0.15625 to 0.15625
- expert_down: bfloat16 [4, 512, 1536], P('ep', 'req'), may hold values from -0.25 to 0.25
Outputs:
- hidden_out: bfloat16 [16, 512, 1536], P('req', None, 'ep')
- key_cache_out: bfloat16 [16, 8, 2560, 64], P('req', 'ep')
- value_cache_out: bfloat16 [16, 8, 2560, 64], P('req', 'ep')
Inputs may be any that keep to these rules, and one draw needn't show every extreme that they name: Slot s holds request request_order[s]; every request is held by one slot. `cached_lengths`: the longest cached length is exactly 2048. `expert_ids`: each token names 8 different experts; among the 512 tokens of one slot no expert is named by more than 192 tokens, a bound that some block reaches.
All inputs are finite; a program needn't handle non-finite values.
Results may differ from a plain program's by a relative error of at most 0.012.
The roundings to bfloat16 on the way count: a program that leaves them out, or rounds other values in their place, can miss the bound.
Values may be sent and summed in bfloat16 or wider, within the bound.
No kernel may reach another device: no remote copies, remote signals or barrier semaphores. Data moves between devices by JAX's collectives and lax.ppermute only.
A program may use at most 128 MiB of HBM per device.

v0:
```python
import jax
import jax.numpy as jnp
from jax import lax
from jax.sharding import PartitionSpec as P

epsilon = 1e-06


def normalize(values, gain):
    return values * lax.rsqrt(jnp.mean(values * values, -1, keepdims=True) + epsilon) * gain


def rotate(values, positions):
    half = values.shape[-1] // 2
    freq = 10000.0 ** (-jnp.arange(half, dtype=jnp.float32) * (2.0 / values.shape[-1]))
    angle = positions.astype(jnp.float32)[:, None] * freq[None, :]
    cosine = jnp.cos(angle)
    sine = jnp.sin(angle)
    first = values[..., :half]
    second = values[..., half:]
    return jnp.concatenate([first * cosine - second * sine, second * cosine + first * sine], -1)


def rounded(values):
    return lax.optimization_barrier(values.astype(jnp.bfloat16)).astype(jnp.float32)


def route_tables(chosen, gate_rows, wanted, capacity):
    hits = chosen[:, :, None] == wanted[None, None, :]
    member = jnp.sum(hits.astype(jnp.int32), 1, dtype=jnp.int32)
    weight = jnp.sum(jnp.where(hits, gate_rows[:, :, None], 0.0), 1)
    place = jnp.cumsum(member, 0, dtype=jnp.int32) - 1
    slots = jnp.arange(capacity, dtype=jnp.int32)
    table = (member.T[:, None, :] == 1) & (place.T[:, None, :] == slots[None, :, None])
    gate_slot = jnp.sum(jnp.where(table, weight.T[:, None, :], 0.0), 2)
    return (table.astype(jnp.bfloat16), gate_slot)


def attend(query, keys, values, length, new_rows):
    query_rows = query.shape[1]
    blocks = keys.shape[1] // new_rows
    limit = length + jnp.arange(query_rows, dtype=jnp.int32) % new_rows
    scale = query.shape[2] ** (-0.5)

    def visit(carry, block):
        running, total, summed = carry
        start = block * new_rows
        key_block = lax.dynamic_slice_in_dim(keys, start, new_rows, 1)
        value_block = lax.dynamic_slice_in_dim(values, start, new_rows, 1)
        scores = (
            jnp.einsum("kqd,kjd->kqj", query, key_block, preferred_element_type=jnp.float32) * scale
        )
        column = start + jnp.arange(new_rows, dtype=jnp.int32)
        visible = column[None, :] <= limit[:, None]
        scores = jnp.where(visible[None], scores, -1e30)
        highest = jnp.maximum(running, jnp.max(scores, -1))
        correction = jnp.exp(running - highest)
        probs = jnp.where(visible[None], jnp.exp(scores - highest[..., None]), 0.0)
        total = total * correction + jnp.sum(probs, -1)
        summed = summed * correction[..., None] + jnp.einsum(
            "kqj,kjd->kqd",
            probs.astype(jnp.bfloat16),
            value_block,
            preferred_element_type=jnp.float32,
        )
        return ((highest, total, summed), None)

    start_state = (
        jnp.full(query.shape[:2], -1e30, jnp.float32),
        jnp.zeros(query.shape[:2], jnp.float32),
        jnp.zeros(query.shape, jnp.float32),
    )
    final, unused = lax.scan(visit, start_state, jnp.arange(blocks, dtype=jnp.int32))
    return final[2] / final[1][..., None]


def on_device(
    hidden,
    key_cache,
    value_cache,
    request_order,
    cached_lengths,
    expert_ids,
    gate_values,
    attn_gain,
    ffn_gain,
    w_query,
    w_key,
    w_value,
    w_out,
    expert_gate,
    expert_up,
    expert_down,
):
    own_rows = hidden[0]
    new_rows = own_rows.shape[0]
    own_width = own_rows.shape[1]
    head_dim = key_cache.shape[3]
    kv_local = key_cache.shape[1]
    heads_local = w_query.shape[1] // head_dim
    group = heads_local // kv_local
    per_device = expert_gate.shape[0]
    devices = lax.axis_size("ep")
    capacity = 3 * new_rows // 8
    everyone = jnp.arange(request_order.shape[0], dtype=jnp.int32)
    request = jnp.sum(jnp.where(everyone == lax.axis_index("req"), request_order, 0))
    length = jnp.sum(jnp.where(everyone == request, cached_lengths, 0))
    rows_whole = lax.all_gather(own_rows, "ep", axis=1, tiled=True)
    width = rows_whole.shape[1]
    normed = normalize(rows_whole.astype(jnp.float32), attn_gain).astype(jnp.bfloat16)
    query = jnp.dot(normed, w_query, preferred_element_type=jnp.float32)
    key_new = jnp.dot(normed, w_key, preferred_element_type=jnp.float32)
    value_new = jnp.dot(normed, w_value, preferred_element_type=jnp.float32)
    positions = length + jnp.arange(new_rows, dtype=jnp.int32)
    query = rotate(
        query.reshape(new_rows, heads_local, head_dim).transpose(1, 0, 2), positions
    ).astype(jnp.bfloat16)
    query = query.reshape(kv_local, group * new_rows, head_dim)
    key_new = rotate(
        key_new.reshape(new_rows, kv_local, head_dim).transpose(1, 0, 2), positions
    ).astype(jnp.bfloat16)
    value_new = (
        value_new.reshape(new_rows, kv_local, head_dim).transpose(1, 0, 2).astype(jnp.bfloat16)
    )
    zero = jnp.zeros((), jnp.int32)
    keys = lax.dynamic_update_slice(key_cache[0], key_new, (zero, length, zero))
    values = lax.dynamic_update_slice(value_cache[0], value_new, (zero, length, zero))
    attended = attend(query, keys, values, length, new_rows)
    attended = (
        attended.reshape(heads_local, new_rows, head_dim)
        .transpose(1, 0, 2)
        .reshape(new_rows, heads_local * head_dim)
        .astype(jnp.bfloat16)
    )
    partial_value = rounded(jnp.dot(attended, w_out, preferred_element_type=jnp.float32))
    head_sum = lax.psum_scatter(
        partial_value.astype(jnp.bfloat16), "ep", scatter_dimension=1, tiled=True
    ).astype(jnp.float32)
    mixed = (own_rows.astype(jnp.float32) + head_sum).astype(jnp.bfloat16)
    mixed_f = mixed.astype(jnp.float32)
    chosen = expert_ids[0]
    gate_rows = gate_values[0]
    first = lax.axis_index("ep") * per_device
    squares = jnp.sum(mixed_f * mixed_f, -1)
    totals = lax.psum(squares, "ep")
    local_gain = lax.dynamic_slice_in_dim(ffn_gain, lax.axis_index("ep") * own_width, own_width)
    normed_cols = (mixed_f * lax.rsqrt(totals / width + epsilon)[:, None] * local_gain).astype(
        jnp.bfloat16
    )
    table_all, gate_all = route_tables(
        chosen, gate_rows, jnp.arange(per_device * devices, dtype=jnp.int32), capacity
    )
    buffers = jnp.einsum(
        "ect,td->ecd", table_all, normed_cols, preferred_element_type=jnp.float32
    ).astype(jnp.bfloat16)
    inputs = lax.all_to_all(buffers, "ep", split_axis=0, concat_axis=2, tiled=True)
    gate_own = lax.dynamic_slice_in_dim(gate_all, first, per_device, 0)
    columns = inputs
    gate_next = jnp.einsum(
        "ecd,edf->ecf",
        columns,
        lax.all_gather(expert_gate, "req", axis=1, tiled=True),
        preferred_element_type=jnp.float32,
    )
    up_next = jnp.einsum(
        "ecd,edf->ecf",
        columns,
        lax.all_gather(expert_up, "req", axis=1, tiled=True),
        preferred_element_type=jnp.float32,
    )
    hidden_act = (jax.nn.silu(gate_next) * up_next).astype(jnp.bfloat16)
    columns = hidden_act
    output = jnp.einsum(
        "ecf,efd->ecd",
        columns,
        lax.all_gather(expert_down, "req", axis=1, tiled=True),
        preferred_element_type=jnp.float32,
    )
    contrib = (output * gate_own[..., None]).astype(jnp.bfloat16)
    returned = lax.all_to_all(contrib, "ep", split_axis=2, concat_axis=0, tiled=True)
    per_expert = jnp.einsum("ect,ecd->etd", table_all, returned, preferred_element_type=jnp.float32)
    grouped = rounded(jnp.sum(per_expert.reshape(devices, per_device, new_rows, own_width), 1))
    expert_sum = jnp.sum(grouped, 0)
    result = (mixed_f + expert_sum).astype(jnp.bfloat16)
    return (result[None], keys[None], values[None])


def solution(mesh):
    in_specs = (
        P("req", None, "ep"),
        P("req", "ep", None, None),
        P("req", "ep", None, None),
        P(),
        P(),
        P("req", None, None),
        P("req", None, None),
        P(),
        P(),
        P(None, "ep"),
        P(None, "ep"),
        P(None, "ep"),
        P("ep", None),
        P("ep", "req", None),
        P("ep", "req", None),
        P("ep", "req", None),
    )
    out_specs = (P("req", None, "ep"), P("req", "ep", None, None), P("req", "ep", None, None))
    return jax.shard_map(
        on_device, mesh=mesh, in_specs=in_specs, out_specs=out_specs, check_vma=False
    )
```

profile of v0, /device:TPU:0, one launch (start us, length us, event | category | flops | bytes accessed | tf_op | source)
XLA Modules:
  0.0 390.4 jit_solution(1194642636352865639)
XLA Ops:
  8.1 2.6 copy.81
  10.7 1.1 copy.82
  12.5 1.3 fusion.60
  16.7 25.2 %all-gather.12.cloned.1.call-done = bf16[1,512,1536]{2,1,0:T(8,128)(2,1)} async-done(((bf16[1,512,768]{2,1,0:T(8,128)(2,1)}), bf16[1,512,1536]{2,1,0:T(8,128)(2,1)}) %all-gather.12.cloned.1.call-update) | async-done | bytes 1572880 | tf_op jit(solution)/shard_map/all_gather | solution.py:108
  41.8 1.9 fusion.24
  43.8 2.1 fusion.66
  46.0 1.6 fusion.64
  47.5 1.0 subtract_convert_fusion
  48.8 1.1 concatenate.14
  49.8 1.2 copy.52
  51.0 1.1 concatenate.15
  52.1 1.6 pad_maximum_fusion
  53.8 1.0 copy.53
  54.8 4.0 %dynamic_update_slice.6 = bf16[4,2560,64]{1,2,0:T(8,128)(2,1)} dynamic-update-slice(bf16[4,2560,64]{1,2,0:T(8,128)(2,1)} %bitcast.102, bf16[4,512,64]{1,2,0:T(8,128)(2,1)S(1)} %pad_maximum_fusion.1, s32[]{:T(128)} %constant.31.clone.1, s32[]{:T(128)S(6)} %select_n.46, s32[]{:T(128)} %constant.31.clone.1) | dynamic-update-slice | bytes 524292 | tf_op jit(solution)/shard_map/dynamic_update_slice | solution.py:126
  58.8 2.4 convolution_convert_fusion.1
  61.1 3.8 dynamic_update_slice.7
  64.9 123.9 %while.15 = (s32[]{:T(128)}, f32[4,1536]{1,0:T(4,128)S(1)}, f32[4,1536]{1,0:T(4,128)S(1)}, f32[4,1536,64]{1,2,0:T(8,128)}, s32[5]{0:T(128)S(1)}, /*index=5*/bf16...) while((s32[]{:T(128)}, f32[4,1536]{1,0:T(4,128)S(1)}, ...), condition=%wide.region_6.7_spmd.clone, body=%wide.region_3.6_spmd.clone.sunk | while | flops 848208896 | bytes 96092400 | solution.py:73
  64.9 0.7 dynamic_slice.33
  67.5 8.1 %fusion.93 = (f32[4,1536]{1,0:T(4,128)S(1)}, f32[4,512,1536]{2,1,0:T(8,128)}) fusion(pred[1536,512]{0,1:T(8,128)(4,1)S(1)} %broadcast_compare_fusion.3, bf16[4,1536,64]{1,2,0:T(8,128)(2,1)} %get-tuple-element.236, bf16[4,2560,64]{1,2,0:T(8,128)(2,1)} %get-tuple-element.235, s32[]{:T(128)S(6)} %select_n.102), kind=kOutput, calls=%fused_computation.3.clone.1 | convolution fusion | flops 412084224 | bytes 14442500 | tf_op jit(solution)/shard_map/while/body/eval_jaxpr/kqd,kjd->kqj/dot_general | solution.py:51
  75.6 6.9 %fusion.94 = f32[4,1536]{1,0:T(4,128)S(1)} fusion(f32[4,512,1536]{2,1,0:T(8,128)} %get-tuple-element.201, f32[4,1536]{1,0:T(4,128)S(1)} %select_maximum_fusion.2, pred[1536,512]{0,1:T(8,128)(4,1)S(1)} %broadcast_compare_fusion.3), kind=kLoop, calls=%fused_computation.5.clone.1 | loop fusion | flops 15722496 | bytes 13418496 | tf_op jit(solution)/shard_map/while/body/eval_jaxpr/reduce_sum | solution.py:59
  82.5 1.4 copy-done.1
  83.8 5.7 %fusion.96 = f32[4,1536,64]{1,2,0:T(8,128)} fusion(f32[4,512,1536]{2,1,0:T(8,128)S(1)} %copy-done.1, f32[4,1536]{1,0:T(4,128)S(1)} %select_maximum_fusion.2, pred[1536,512]{0,1:T(8,128)(4,1)S(1)} %broadcast_compare_fusion.3, f32[4,1536,64]{1,2,0:T(8,128)} %get-tuple-element.220, f32[4,1536]{1,0:T(4,128)S(1)} %get-tuple-element.203, pred[]{:T(512)S(6)} %compare.4, ...), kind=kOutput, calls=%fused_computation.8.clone.1 | convolution fusion | flops 419561472 | bytes 16826372 | tf_op jit(solution)/shard_map/while/body/eval_jaxpr/kqj,kjd->kqd/dot_general | solution.py:60
  89.5 0.7 dynamic_slice.33
  92.1 8.1 %fusion.93 = (f32[4,1536]{1,0:T(4,128)S(1)}, f32[4,512,1536]{2,1,0:T(8,128)}) fusion(pred[1536,512]{0,1:T(8,128)(4,1)S(1)} %broadcast_compare_fusion.3, bf16[4,1536,64]{1,2,0:T(8,128)(2,1)} %get-tuple-element.236, bf16[4,2560,64]{1,2,0:T(8,128)(2,1)} %get-tuple-element.235, s32[]{:T(128)S(6)} %select_n.102), kind=kOutput, calls=%fused_computation.3.clone.1 | convolution fusion | flops 412084224 | bytes 14442500 | tf_op jit(solution)/shard_map/while/body/eval_jaxpr/kqd,kjd->kqj/dot_general | solution.py:51
  100.1 6.9 %fusion.94 = f32[4,1536]{1,0:T(4,128)S(1)} fusion(f32[4,512,1536]{2,1,0:T(8,128)} %get-tuple-element.201, f32[4,1536]{1,0:T(4,128)S(1)} %select_maximum_fusion.2, pred[1536,512]{0,1:T(8,128)(4,1)S(1)} %broadcast_compare_fusion.3), kind=kLoop, calls=%fused_computation.5.clone.1 | loop fusion | flops 15722496 | bytes 13418496 | tf_op jit(solution)/shard_map/while/body/eval_jaxpr/reduce_sum | solution.py:59
  107.0 1.4 copy-done.1
  108.4 6.0 %fusion.96 = f32[4,1536,64]{1,2,0:T(8,128)} fusion(f32[4,512,1536]{2,1,0:T(8,128)S(1)} %copy-done.1, f32[4,1536]{1,0:T(4,128)S(1)} %select_maximum_fusion.2, pred[1536,512]{0,1:T(8,128)(4,1)S(1)} %broadcast_compare_fusion.3, f32[4,1536,64]{1,2,0:T(8,128)} %get-tuple-element.220, f32[4,1536]{1,0:T(4,128)S(1)} %get-tuple-element.203, pred[]{:T(512)S(6)} %compare.4, ...), kind=kOutput, calls=%fused_computation.8.clone.1 | convolution fusion | flops 419561472 | bytes 16826372 | tf_op jit(solution)/shard_map/while/body/eval_jaxpr/kqj,kjd->kqd/dot_general | solution.py:60
  114.4 0.7 dynamic_slice.33
  116.9 8.1 %fusion.93 = (f32[4,1536]{1,0:T(4,128)S(1)}, f32[4,512,1536]{2,1,0:T(8,128)}) fusion(pred[1536,512]{0,1:T(8,128)(4,1)S(1)} %broadcast_compare_fusion.3, bf16[4,1536,64]{1,2,0:T(8,128)(2,1)} %get-tuple-element.236, bf16[4,2560,64]{1,2,0:T(8,128)(2,1)} %get-tuple-element.235, s32[]{:T(128)S(6)} %select_n.102), kind=kOutput, calls=%fused_computation.3.clone.1 | convolution fusion | flops 412084224 | bytes 14442500 | tf_op jit(solution)/shard_map/while/body/eval_jaxpr/kqd,kjd->kqj/dot_general | solution.py:51
  125.0 6.9 %fusion.94 = f32[4,1536]{1,0:T(4,128)S(1)} fusion(f32[4,512,1536]{2,1,0:T(8,128)} %get-tuple-element.201, f32[4,1536]{1,0:T(4,128)S(1)} %select_maximum_fusion.2, pred[1536,512]{0,1:T(8,128)(4,1)S(1)} %broadcast_compare_fusion.3), kind=kLoop, calls=%fused_computation.5.clone.1 | loop fusion | flops 15722496 | bytes 13418496 | tf_op jit(solution)/shard_map/while/body/eval_jaxpr/reduce_sum | solution.py:59
  131.9 1.4 copy-done.1
  133.2 6.0 %fusion.96 = f32[4,1536,64]{1,2,0:T(8,128)} fusion(f32[4,512,1536]{2,1,0:T(8,128)S(1)} %copy-done.1, f32[4,1536]{1,0:T(4,128)S(1)} %select_maximum_fusion.2, pred[1536,512]{0,1:T(8,128)(4,1)S(1)} %broadcast_compare_fusion.3, f32[4,1536,64]{1,2,0:T(8,128)} %get-tuple-element.220, f32[4,1536]{1,0:T(4,128)S(1)} %get-tuple-element.203, pred[]{:T(512)S(6)} %compare.4, ...), kind=kOutput, calls=%fused_computation.8.clone.1 | convolution fusion | flops 419561472 | bytes 16826372 | tf_op jit(solution)/shard_map/while/body/eval_jaxpr/kqj,kjd->kqd/dot_general | solution.py:60
  139.2 0.7 dynamic_slice.33
  141.7 8.1 %fusion.93 = (f32[4,1536]{1,0:T(4,128)S(1)}, f32[4,512,1536]{2,1,0:T(8,128)}) fusion(pred[1536,512]{0,1:T(8,128)(4,1)S(1)} %broadcast_compare_fusion.3, bf16[4,1536,64]{1,2,0:T(8,128)(2,1)} %get-tuple-element.236, bf16[4,2560,64]{1,2,0:T(8,128)(2,1)} %get-tuple-element.235, s32[]{:T(128)S(6)} %select_n.102), kind=kOutput, calls=%fused_computation.3.clone.1 | convolution fusion | flops 412084224 | bytes 14442500 | tf_op jit(solution)/shard_map/while/body/eval_jaxpr/kqd,kjd->kqj/dot_general | solution.py:51
  149.8 6.9 %fusion.94 = f32[4,1536]{1,0:T(4,128)S(1)} fusion(f32[4,512,1536]{2,1,0:T(8,128)} %get-tuple-element.201, f32[4,1536]{1,0:T(4,128)S(1)} %select_maximum_fusion.2, pred[1536,512]{0,1:T(8,128)(4,1)S(1)} %broadcast_compare_fusion.3), kind=kLoop, calls=%fused_computation.5.clone.1 | loop fusion | flops 15722496 | bytes 13418496 | tf_op jit(solution)/shard_map/while/body/eval_jaxpr/reduce_sum | solution.py:59
  156.7 1.4 copy-done.1
  158.1 6.0 %fusion.96 = f32[4,1536,64]{1,2,0:T(8,128)} fusion(f32[4,512,1536]{2,1,0:T(8,128)S(1)} %copy-done.1, f32[4,1536]{1,0:T(4,128)S(1)} %select_maximum_fusion.2, pred[1536,512]{0,1:T(8,128)(4,1)S(1)} %broadcast_compare_fusion.3, f32[4,1536,64]{1,2,0:T(8,128)} %get-tuple-element.220, f32[4,1536]{1,0:T(4,128)S(1)} %get-tuple-element.203, pred[]{:T(512)S(6)} %compare.4, ...), kind=kOutput, calls=%fused_computation.8.clone.1 | convolution fusion | flops 419561472 | bytes 16826372 | tf_op jit(solution)/shard_map/while/body/eval_jaxpr/kqj,kjd->kqd/dot_general | solution.py:60
  164.1 0.7 dynamic_slice.33
  166.6 8.1 %fusion.93 = (f32[4,1536]{1,0:T(4,128)S(1)}, f32[4,512,1536]{2,1,0:T(8,128)}) fusion(pred[1536,512]{0,1:T(8,128)(4,1)S(1)} %broadcast_compare_fusion.3, bf16[4,1536,64]{1,2,0:T(8,128)(2,1)} %get-tuple-element.236, bf16[4,2560,64]{1,2,0:T(8,128)(2,1)} %get-tuple-element.235, s32[]{:T(128)S(6)} %select_n.102), kind=kOutput, calls=%fused_computation.3.clone.1 | convolution fusion | flops 412084224 | bytes 14442500 | tf_op jit(solution)/shard_map/while/body/eval_jaxpr/kqd,kjd->kqj/dot_general | solution.py:51
  174.7 6.9 %fusion.94 = f32[4,1536]{1,0:T(4,128)S(1)} fusion(f32[4,512,1536]{2,1,0:T(8,128)} %get-tuple-element.201, f32[4,1536]{1,0:T(4,128)S(1)} %select_maximum_fusion.2, pred[1536,512]{0,1:T(8,128)(4,1)S(1)} %broadcast_compare_fusion.3), kind=kLoop, calls=%fused_computation.5.clone.1 | loop fusion | flops 15722496 | bytes 13418496 | tf_op jit(solution)/shard_map/while/body/eval_jaxpr/reduce_sum | solution.py:59
  181.6 1.4 copy-done.1
  182.9 6.0 %fusion.96 = f32[4,1536,64]{1,2,0:T(8,128)} fusion(f32[4,512,1536]{2,1,0:T(8,128)S(1)} %copy-done.1, f32[4,1536]{1,0:T(4,128)S(1)} %select_maximum_fusion.2, pred[1536,512]{0,1:T(8,128)(4,1)S(1)} %broadcast_compare_fusion.3, f32[4,1536,64]{1,2,0:T(8,128)} %get-tuple-element.220, f32[4,1536]{1,0:T(4,128)S(1)} %get-tuple-element.203, pred[]{:T(512)S(6)} %compare.4, ...), kind=kOutput, calls=%fused_computation.8.clone.1 | convolution fusion | flops 419561472 | bytes 16826372 | tf_op jit(solution)/shard_map/while/body/eval_jaxpr/kqj,kjd->kqd/dot_general | solution.py:60
  188.9 1.5 divide_convert_fusion
  190.4 1.5 copy.54
  191.9 1.8 convert_element_type.91
  194.2 2.6 convolution_convert_fusion
  198.6 1.2 reduce-window.6
  200.4 22.6 %reduce-scatter.2.cloned.1.call-done = bf16[512,768]{1,0:T(8,128)(2,1)} async-done(((bf16[512,1536]{1,0:T(8,128)(2,1)}), bf16[512,768]{1,0:T(8,128)(2,1)}) %reduce-scatter.2.cloned.1.call-update) | async-done | bytes 786448 | tf_op jit(solution)/shard_map/reduce_scatter | solution.py:136
  223.1 1.5 fusion.28
  224.5 5.2 %psum.7 = f32[512]{0:T(512)S(1)} all-reduce(f32[512]{0:T(512)S(1)} %fusion.28), channel_id=1, replica_groups=mesh['req'=16,'ep'=2] {'ep'}, use_global_device_ids=true, to_apply=%region_12.13 | all-reduce | flops 512 | bytes 4096 | tf_op jit(solution)/shard_map/psum | solution.py:145
  229.7 3.2 fusion.40
  232.9 4.6 %all-to-all-start = ((bf16[4,192,768]{2,1,0:T(8,128)(2,1)}), bf16[4,192,768]{2,1,0:T(8,128)(2,1)}, u32[]{:S(2)}, u32[]{:S(2)}) async-start(bf16[4,192,768]{2,1,0:T(8,128)(2,1)} %fusion.40), calls=%async_computation.1 | async-start | bytes 2359296 | tf_op jit(solution)/shard_map/all_to_all | solution.py:156
  238.0 14.2 %all-to-all-done = bf16[4,192,768]{2,1,0:T(8,128)(2,1)} async-done(((bf16[4,192,768]{2,1,0:T(8,128)(2,1)}), bf16[4,192,768]{2,1,0:T(8,128)(2,1)}, u32[]{:S(2)}, u32[]{:S(2)}) %all-to-all-start) | async-done | bytes 1179680 | tf_op jit(solution)/shard_map/all_to_all | solution.py:156
  252.2 2.4 copy.61
  254.6 3.9 %fusion.68 = f32[2,192,512]{2,1,0:T(8,128)} fusion(bf16[2,192,1536]{2,1,0:T(8,128)(2,1)} %bitcast.104, bf16[2,1536,512]{2,1,0:T(8,128)(2,1)} %all-gather.6.cloned.1.call-done), kind=kOutput, calls=%fused_computation.100 | convolution fusion | flops 603979776 | bytes 5111808 | tf_op jit(solution)/shard_map/ecd,edf->ecf/dot_general | solution.py:159
  258.5 32.5 %all-gather.10.cloned.1.call-done = bf16[2,512,1536]{2,1,0:T(8,128)(2,1)} async-done(((bf16[2,32,1536]{2,1,0:T(8,128)(2,1)}), bf16[2,512,1536]{2,1,0:T(8,128)(2,1)}) %all-gather.10.cloned.1.call-update) | async-done | bytes 3145744 | tf_op jit(solution)/shard_map/all_gather | solution.py:176
  291.0 46.1 %all-gather.8.cloned.1.call-done = bf16[2,1536,512]{2,1,0:T(8,128)(2,1)} async-done(((bf16[2,96,512]{2,1,0:T(8,128)(2,1)}), bf16[2,1536,512]{2,1,0:T(8,128)(2,1)}) %all-gather.8.cloned.1.call-update) | async-done | bytes 3145744 | tf_op jit(solution)/shard_map/all_gather | solution.py:168
  337.2 5.9 %fusion.27 = bf16[2,192,1536]{2,1,0:T(8,128)(2,1)} fusion(bf16[2,512,1536]{2,1,0:T(8,128)(2,1)} %all-gather.10.cloned.1.call-done, f32[2,192]{1,0:T(2,128)S(1)} %constant_dynamic-slice_fusion, bf16[2,192,1536]{2,1,0:T(8,128)(2,1)} %bitcast.105, bf16[2,1536,512]{2,1,0:T(8,128)(2,1)} %all-gather.8.cloned.1.call-done, f32[2,192,512]{2,1,0:T(8,128)} %fusion.68), kind=kOutput, calls=%fused_computation.39 | convolution fusion | flops 1210318848 | bytes 9438720 | tf_op jit(solution)/shard_map/ecf,efd->ecd/dot_general | solution.py:173
  343.1 4.8 %copy.57 = bf16[2,192,1536]{1,0,2:T(2,128)(2,1)} copy(bf16[2,192,1536]{2,1,0:T(8,128)(2,1)} %fusion.27) | data formatting | bytes 2359296 | tf_op jit(solution)/shard_map/convert_element_type | solution.py:179
  347.9 25.2 %all_to_all.36 = bf16[2,192,1536]{1,0,2:T(2,128)(2,1)} all-to-all(bf16[2,192,1536]{1,0,2:T(2,128)(2,1)} %copy.57), channel_id=1, replica_groups=mesh['req'=16,'ep'=2] {'ep'}, dimensions={2} | all-to-all | bytes 2359296 | tf_op jit(solution)/shard_map/all_to_all | solution.py:180
  373.1 4.9 %copy.58 = bf16[2,192,2,768]{3,1,0,2:T(8,128)(2,1)} copy(bf16[2,192,2,768]{1,0,3,2:T(2,128)(2,1)} %bitcast.101) | data formatting | bytes 2359296 | tf_op jit(solution)/shard_map/all_to_all | solution.py:180
  378.0 2.5 bitcast_reduce_fusion
  380.8 0.9 copy-done.3
  381.6 1.2 fusion.44
  (95 shorter events, 11.6 us)
Async XLA Ops:
  8.0 186.2 %copy-start = (bf16[768,1536]{1,0:T(8,128)(2,1)S(1)}, bf16[768,1536]{1,0:T(8,128)(2,1)}, u32[]{:S(2)}) copy-start(bf16[768,1536]{1,0:T(8,128)(2,1)} %param.30) | copy-start | bytes 7077892
  8.0 33.8 %all-gather.12.cloned.1.call-start = ((), (), s32[]{:S(2)}) async-start(), calls=%async_computation.7 | async-start | bytes 2359296 | tf_op jit(solution)/shard_map/all_gather | solution.py:108
  8.1 2.6 copy-start.5
  10.7 1.2 copy-start.11
  10.7 1.8 copy-start.12
  11.8 32.0 %copy-start.10 = (f32[1536]{0:T(1024)S(1)}, f32[1536]{0:T(1024)}, u32[]{:S(2)}) copy-start(f32[1536]{0:T(1024)} %param.25) | copy-start | bytes 18436
  11.8 211.3 %reduce-scatter.2.cloned.1.call-start = ((), (), s32[]{:S(2)}) async-start(), calls=%async_computation.3 | async-start | bytes 2359296 | tf_op jit(solution)/shard_map/reduce_scatter | solution.py:136
  41.8 1.9 copy-start.4
  43.8 2.2 copy-start.9
  75.6 8.3 %copy-start.1 = (f32[4,512,1536]{2,1,0:T(8,128)S(1)}, f32[4,512,1536]{2,1,0:T(8,128)}, u32[]{:S(2)}) copy-start(f32[4,512,1536]{2,1,0:T(8,128)} %get-tuple-element.201) | copy-start | bytes 37748740 | tf_op jit(solution)/shard_map/while
  100.1 8.3 %copy-start.1 = (f32[4,512,1536]{2,1,0:T(8,128)S(1)}, f32[4,512,1536]{2,1,0:T(8,128)}, u32[]{:S(2)}) copy-start(f32[4,512,1536]{2,1,0:T(8,128)} %get-tuple-element.201) | copy-start | bytes 37748740 | tf_op jit(solution)/shard_map/while
  125.0 8.3 %copy-start.1 = (f32[4,512,1536]{2,1,0:T(8,128)S(1)}, f32[4,512,1536]{2,1,0:T(8,128)}, u32[]{:S(2)}) copy-start(f32[4,512,1536]{2,1,0:T(8,128)} %get-tuple-element.201) | copy-start | bytes 37748740 | tf_op jit(solution)/shard_map/while
  149.8 8.3 %copy-start.1 = (f32[4,512,1536]{2,1,0:T(8,128)S(1)}, f32[4,512,1536]{2,1,0:T(8,128)}, u32[]{:S(2)}) copy-start(f32[4,512,1536]{2,1,0:T(8,128)} %get-tuple-element.201) | copy-start | bytes 37748740 | tf_op jit(solution)/shard_map/while
  174.7 8.3 %copy-start.1 = (f32[4,512,1536]{2,1,0:T(8,128)S(1)}, f32[4,512,1536]{2,1,0:T(8,128)}, u32[]{:S(2)}) copy-start(f32[4,512,1536]{2,1,0:T(8,128)} %get-tuple-element.201) | copy-start | bytes 37748740 | tf_op jit(solution)/shard_map/while
  196.8 1.8 copy-start.6
  196.8 3.5 copy-start.8
  196.8 26.3 %copy-start.2 = (bf16[1,512,768]{2,1,0:T(8,128)(2,1)S(1)}, bf16[1,512,768]{2,1,0:T(8,128)(2,1)}, u32[]{:S(2)}) copy-start(bf16[1,512,768]{2,1,0:T(8,128)(2,1)} %param.18) | copy-start | bytes 2359300
  196.8 57.7 %all-gather.6.cloned.1.call-start = ((), (), s32[]{:S(2)}) async-start(), calls=%async_computation.4 | async-start | bytes 3342336 | tf_op jit(solution)/shard_map/all_gather | solution.py:162
  197.4 93.6 %all-gather.10.cloned.1.call-start = ((), (), s32[]{:S(2)}) async-start(), calls=%async_computation.6 | async-start | bytes 3342336 | tf_op jit(solution)/shard_map/all_gather | solution.py:176
  198.0 139.2 %all-gather.8.cloned.1.call-start = ((), (), s32[]{:S(2)}) async-start(), calls=%async_computation.5 | async-start | bytes 3342336 | tf_op jit(solution)/shard_map/all_gather | solution.py:168
  232.9 4.6 %copy-start.7 = (f32[1,512,8]{1,2,0:T(8,128)S(1)}, f32[1,512,8]{1,2,0:T(8,128)}, u32[]{:S(2)}) copy-start(f32[1,512,8]{1,2,0:T(8,128)} %param.24) | copy-start | bytes 49156
  232.9 19.2 %all-to-all-start = ((bf16[4,192,768]{2,1,0:T(8,128)(2,1)}), bf16[4,192,768]{2,1,0:T(8,128)(2,1)}, u32[]{:S(2)}, u32[]{:S(2)}) async-start(bf16[4,192,768]{2,1,0:T(8,128)(2,1)} %fusion.40), calls=%async_computation.1 | async-start | bytes 2359296 | tf_op jit(solution)/shard_map/all_to_all | solution.py:156
  380.5 1.1 copy-start.3
Sparse Core Ops, SparseCore 0:
  11.9 29.8 all-gather.11
  197.0 26.0 reduce-scatter.1
Sparse Core Ops, SparseCore 1:
  199.6 45.5 all-gather.5
  247.3 43.7 all-gather.9
  293.5 43.7 all-gather.7
where the time goes:
time: 392 us; the launch traced here: 390 us
  waiting for transfers between devices  142 us (36%)
  matrix products  93.9 us (24%)
  other arithmetic  54.2 us (14%)
  local copies, waits for them, and re-layouts  43.3 us (11%)
  blocking collectives  30.4 us (8%)
  between operations  17.8 us (5%)
  starting transfers between devices  4.8 us (1%)
    all_gather x1, waiting for transfers between devices, on_device(): lax.all_gather(expert_up, 'req', axis=1, tiled=True)  46.1 us
    dot_general x5, matrix products, visit(): jnp.einsum('kqd,kjd->kqj', query, key_block, preferred_element_type=jnp.f...  40.3 us
    reduce_sum x5, other arithmetic, visit(): total = total * correction + jnp.sum(probs, -1)  34.3 us
    all_gather x1, waiting for transfers between devices, on_device(): lax.all_gather(expert_down, 'req', axis=1, tiled=True)  32.5 us
    dot_general x5, matrix products, visit(): jnp.einsum('kqj,kjd->kqd', probs.astype(jnp.bfloat16), value_block, prefe...  29.5 us
    all_to_all x1, blocking collectives, on_device(): lax.all_to_all(contrib, 'ep', split_axis=2, concat_axis=0, tiled=True)  25.2 us
    all_gather x1, waiting for transfers between devices, on_device(): rows_whole = lax.all_gather(own_rows, 'ep', axis=1, tiled=True)  25.2 us
    reduce_scatter x1, waiting for transfers between devices, on_device(): lax.psum_scatter(partial_value.astype(jnp.bfloat16), 'ep', scatter_dimens...  22.6 us
  transfers between devices with their start and end apart: 6, of which 5 were waited for; matrix products, arithmetic and copies ran while one was open for 4% of the time, Pallas kernels for 0%

commit v1 on v0

--- a/solution.py
+++ b/solution.py
@@ -177,7 +177,10 @@
         preferred_element_type=jnp.float32,
     )
     contrib = (output * gate_own[..., None]).astype(jnp.bfloat16)
-    returned = lax.all_to_all(contrib, "ep", split_axis=2, concat_axis=0, tiled=True)
+    n_dev = lax.axis_size("ep")
+    parts = jnp.stack(jnp.split(contrib, n_dev, axis=2), axis=0)
+    parts = lax.all_to_all(parts, "ep", split_axis=0, concat_axis=0)
+    returned = jnp.concatenate(parts, axis=0)
     per_expert = jnp.einsum("ect,ecd->etd", table_all, returned, preferred_element_type=jnp.float32)
     grouped = rounded(jnp.sum(per_expert.reshape(devices, per_device, new_rows, own_width), 1))
     expert_sum = jnp.sum(grouped, 0)

time: 392 us -> 375 us (0.957)
  local copies, waits for them, and re-layouts: 43.3 us -> 34.9 us
  blocking collectives: 30.4 us -> 23.3 us
    all_to_all x1, blocking collectives: 25.2 us -> 18.2 us  [on_device(): parts = lax.all_to_all(parts, 'ep', split_axis=0, concat_axis=0)]
    all_to_all x1 -> x0, local copies, waits for them, and re-layouts: 4.89 us -> none  [on_device(): lax.all_to_all(contrib, 'ep', split_axis=2, concat_axis=0, tiled=True)]
    convert_element_type x1 -> x0, local copies, waits for them, and re-layouts: 4.83 us -> none  [on_device(): contrib = (output * gate_own[..., None]).astype(jnp.bfloat16)]
where the time goes in v1:
time: 375 us; the launch traced here: 374 us
  waiting for transfers between devices  142 us (38%)
  matrix products  92.5 us (25%)
  other arithmetic  54.3 us (14%)
  local copies, waits for them, and re-layouts  34.9 us (9%)
  blocking collectives  23.3 us (6%)
  between operations  17.8 us (5%)
  starting transfers between devices  4.8 us (1%)
    all_gather x1, waiting for transfers between devices, on_device(): lax.all_gather(expert_up, 'req', axis=1, tiled=True)  46.1 us
    dot_general x5, matrix products, visit(): jnp.einsum('kqd,kjd->kqj', query, key_block, preferred_element_type=jnp.f...  40.3 us
    reduce_sum x5, other arithmetic, visit(): total = total * correction + jnp.sum(probs, -1)  34.3 us
    all_gather x1, waiting for transfers between devices, on_device(): lax.all_gather(expert_down, 'req', axis=1, tiled=True)  32.5 us
    dot_general x5, matrix products, visit(): jnp.einsum('kqj,kjd->kqd', probs.astype(jnp.bfloat16), value_block, prefe...  29.5 us
    all_gather x1, waiting for transfers between devices, on_device(): rows_whole = lax.all_gather(own_rows, 'ep', axis=1, tiled=True)  25.2 us
    reduce_scatter x1, waiting for transfers between devices, on_device(): lax.psum_scatter(partial_value.astype(jnp.bfloat16), 'ep', scatter_dimens...  22.6 us
    all_to_all x1, blocking collectives, on_device(): parts = lax.all_to_all(parts, 'ep', split_axis=0, concat_axis=0)  18.2 us
  transfers between devices with their start and end apart: 6, of which 5 were waited for; matrix products, arithmetic and copies ran while one was open for 4% of the time, Pallas kernels for 0%

profile of v1, /device:TPU:0, one launch (start us, length us, event | category | flops | bytes accessed | tf_op | source)
XLA Modules:
  0.0 373.6 jit_solution(6762870034929929859)
XLA Ops:
  8.1 2.6 copy.65
  10.7 1.1 copy.66
  12.5 1.3 fusion.60
  16.7 25.2 %all-gather.12.cloned.1.call-done = bf16[1,512,1536]{2,1,0:T(8,128)(2,1)} async-done(((bf16[1,512,768]{2,1,0:T(8,128)(2,1)}), bf16[1,512,1536]{2,1,0:T(8,128)(2,1)}) %all-gather.12.cloned.1.call-update) | async-done | bytes 1572880 | tf_op jit(solution)/shard_map/all_gather | solution.py:108
  41.8 1.9 fusion.24
  43.8 2.1 fusion.66
  46.0 1.6 fusion.64
  47.5 1.0 subtract_convert_fusion
  48.8 1.1 concatenate.14
  49.8 1.2 copy.38
  51.0 1.1 concatenate.15
  52.1 1.6 pad_maximum_fusion.1
  53.8 1.0 copy.39
  54.8 4.0 %dynamic_update_slice.6 = bf16[4,2560,64]{1,2,0:T(8,128)(2,1)} dynamic-update-slice(bf16[4,2560,64]{1,2,0:T(8,128)(2,1)} %bitcast.102, bf16[4,512,64]{1,2,0:T(8,128)(2,1)S(1)} %pad_maximum_fusion.2, s32[]{:T(128)} %constant.31.clone.1, s32[]{:T(128)S(6)} %select_n.46, s32[]{:T(128)} %constant.31.clone.1) | dynamic-update-slice | bytes 524292 | tf_op jit(solution)/shard_map/dynamic_update_slice | solution.py:126
  58.8 2.4 convolution_convert_fusion.1
  61.1 3.8 %dynamic_update_slice.7 = bf16[4,2560,64]{1,2,0:T(8,128)(2,1)} dynamic-update-slice(bf16[4,2560,64]{1,2,0:T(8,128)(2,1)} %bitcast.109, bf16[4,512,64]{1,2,0:T(8,128)(2,1)S(1)} %bitcast.113, s32[]{:T(128)} %constant.31.clone.1, s32[]{:T(128)S(6)} %select_n.46, s32[]{:T(128)} %constant.31.clone.1) | dynamic-update-slice | bytes 524292 | tf_op jit(solution)/shard_map/dynamic_update_slice | solution.py:127
  64.9 123.9 %while.15 = (s32[]{:T(128)}, f32[4,1536]{1,0:T(4,128)S(1)}, f32[4,1536]{1,0:T(4,128)S(1)}, f32[4,1536,64]{1,2,0:T(8,128)}, s32[5]{0:T(128)S(1)}, /*index=5*/bf16...) while((s32[]{:T(128)}, f32[4,1536]{1,0:T(4,128)S(1)}, ...), condition=%wide.region_6.7_spmd.clone, body=%wide.region_3.6_spmd.clone.sunk | while | flops 848208896 | bytes 96092400 | solution.py:73
  64.9 0.7 dynamic_slice.33
  67.5 8.1 %fusion.93 = (f32[4,1536]{1,0:T(4,128)S(1)}, f32[4,512,1536]{2,1,0:T(8,128)}) fusion(pred[1536,512]{0,1:T(8,128)(4,1)S(1)} %broadcast_compare_fusion.3, bf16[4,1536,64]{1,2,0:T(8,128)(2,1)} %get-tuple-element.229, bf16[4,2560,64]{1,2,0:T(8,128)(2,1)} %get-tuple-element.228, s32[]{:T(128)S(6)} %select_n.102), kind=kOutput, calls=%fused_computation.3.clone.1 | convolution fusion | flops 412084224 | bytes 14442500 | tf_op jit(solution)/shard_map/while/body/eval_jaxpr/kqd,kjd->kqj/dot_general | solution.py:51
  75.6 6.9 %fusion.94 = f32[4,1536]{1,0:T(4,128)S(1)} fusion(f32[4,512,1536]{2,1,0:T(8,128)} %get-tuple-element.194, f32[4,1536]{1,0:T(4,128)S(1)} %select_maximum_fusion.2, pred[1536,512]{0,1:T(8,128)(4,1)S(1)} %broadcast_compare_fusion.3), kind=kLoop, calls=%fused_computation.5.clone.1 | loop fusion | flops 15722496 | bytes 13418496 | tf_op jit(solution)/shard_map/while/body/eval_jaxpr/reduce_sum | solution.py:59
  82.5 1.4 copy-done.1
  83.8 5.7 %fusion.96 = f32[4,1536,64]{1,2,0:T(8,128)} fusion(f32[4,512,1536]{2,1,0:T(8,128)S(1)} %copy-done.1, f32[4,1536]{1,0:T(4,128)S(1)} %select_maximum_fusion.2, pred[1536,512]{0,1:T(8,128)(4,1)S(1)} %broadcast_compare_fusion.3, f32[4,1536,64]{1,2,0:T(8,128)} %get-tuple-element.213, f32[4,1536]{1,0:T(4,128)S(1)} %get-tuple-element.196, pred[]{:T(512)S(6)} %compare.4, ...), kind=kOutput, calls=%fused_computation.8.clone.1 | convolution fusion | flops 419561472 | bytes 16826372 | tf_op jit(solution)/shard_map/while/body/eval_jaxpr/kqj,kjd->kqd/dot_general | solution.py:60
  89.5 0.7 dynamic_slice.33
  90.9 0.6 fusion.92
  92.1 8.1 %fusion.93 = (f32[4,1536]{1,0:T(4,128)S(1)}, f32[4,512,1536]{2,1,0:T(8,128)}) fusion(pred[1536,512]{0,1:T(8,128)(4,1)S(1)} %broadcast_compare_fusion.3, bf16[4,1536,64]{1,2,0:T(8,128)(2,1)} %get-tuple-element.229, bf16[4,2560,64]{1,2,0:T(8,128)(2,1)} %get-tuple-element.228, s32[]{:T(128)S(6)} %select_n.102), kind=kOutput, calls=%fused_computation.3.clone.1 | convolution fusion | flops 412084224 | bytes 14442500 | tf_op jit(solution)/shard_map/while/body/eval_jaxpr/kqd,kjd->kqj/dot_general | solution.py:51
  100.1 6.9 %fusion.94 = f32[4,1536]{1,0:T(4,128)S(1)} fusion(f32[4,512,1536]{2,1,0:T(8,128)} %get-tuple-element.194, f32[4,1536]{1,0:T(4,128)S(1)} %select_maximum_fusion.2, pred[1536,512]{0,1:T(8,128)(4,1)S(1)} %broadcast_compare_fusion.3), kind=kLoop, calls=%fused_computation.5.clone.1 | loop fusion | flops 15722496 | bytes 13418496 | tf_op jit(solution)/shard_map/while/body/eval_jaxpr/reduce_sum | solution.py:59
  107.0 1.4 copy-done.1
  108.4 6.0 %fusion.96 = f32[4,1536,64]{1,2,0:T(8,128)} fusion(f32[4,512,1536]{2,1,0:T(8,128)S(1)} %copy-done.1, f32[4,1536]{1,0:T(4,128)S(1)} %select_maximum_fusion.2, pred[1536,512]{0,1:T(8,128)(4,1)S(1)} %broadcast_compare_fusion.3, f32[4,1536,64]{1,2,0:T(8,128)} %get-tuple-element.213, f32[4,1536]{1,0:T(4,128)S(1)} %get-tuple-element.196, pred[]{:T(512)S(6)} %compare.4, ...), kind=kOutput, calls=%fused_computation.8.clone.1 | convolution fusion | flops 419561472 | bytes 16826372 | tf_op jit(solution)/shard_map/while/body/eval_jaxpr/kqj,kjd->kqd/dot_general | solution.py:60
  114.4 0.7 dynamic_slice.33
  116.9 8.1 %fusion.93 = (f32[4,1536]{1,0:T(4,128)S(1)}, f32[4,512,1536]{2,1,0:T(8,128)}) fusion(pred[1536,512]{0,1:T(8,128)(4,1)S(1)} %broadcast_compare_fusion.3, bf16[4,1536,64]{1,2,0:T(8,128)(2,1)} %get-tuple-element.229, bf16[4,2560,64]{1,2,0:T(8,128)(2,1)} %get-tuple-element.228, s32[]{:T(128)S(6)} %select_n.102), kind=kOutput, calls=%fused_computation.3.clone.1 | convolution fusion | flops 412084224 | bytes 14442500 | tf_op jit(solution)/shard_map/while/body/eval_jaxpr/kqd,kjd->kqj/dot_general | solution.py:51
  125.0 6.9 %fusion.94 = f32[4,1536]{1,0:T(4,128)S(1)} fusion(f32[4,512,1536]{2,1,0:T(8,128)} %get-tuple-element.194, f32[4,1536]{1,0:T(4,128)S(1)} %select_maximum_fusion.2, pred[1536,512]{0,1:T(8,128)(4,1)S(1)} %broadcast_compare_fusion.3), kind=kLoop, calls=%fused_computation.5.clone.1 | loop fusion | flops 15722496 | bytes 13418496 | tf_op jit(solution)/shard_map/while/body/eval_jaxpr/reduce_sum | solution.py:59
  131.9 1.4 copy-done.1
  133.2 6.0 %fusion.96 = f32[4,1536,64]{1,2,0:T(8,128)} fusion(f32[4,512,1536]{2,1,0:T(8,128)S(1)} %copy-done.1, f32[4,1536]{1,0:T(4,128)S(1)} %select_maximum_fusion.2, pred[1536,512]{0,1:T(8,128)(4,1)S(1)} %broadcast_compare_fusion.3, f32[4,1536,64]{1,2,0:T(8,128)} %get-tuple-element.213, f32[4,1536]{1,0:T(4,128)S(1)} %get-tuple-element.196, pred[]{:T(512)S(6)} %compare.4, ...), kind=kOutput, calls=%fused_computation.8.clone.1 | convolution fusion | flops 419561472 | bytes 16826372 | tf_op jit(solution)/shard_map/while/body/eval_jaxpr/kqj,kjd->kqd/dot_general | solution.py:60
  139.2 0.7 dynamic_slice.33
  141.7 8.1 %fusion.93 = (f32[4,1536]{1,0:T(4,128)S(1)}, f32[4,512,1536]{2,1,0:T(8,128)}) fusion(pred[1536,512]{0,1:T(8,128)(4,1)S(1)} %broadcast_compare_fusion.3, bf16[4,1536,64]{1,2,0:T(8,128)(2,1)} %get-tuple-element.229, bf16[4,2560,64]{1,2,0:T(8,128)(2,1)} %get-tuple-element.228, s32[]{:T(128)S(6)} %select_n.102), kind=kOutput, calls=%fused_computation.3.clone.1 | convolution fusion | flops 412084224 | bytes 14442500 | tf_op jit(solution)/shard_map/while/body/eval_jaxpr/kqd,kjd->kqj/dot_general | solution.py:51
  149.8 6.9 %fusion.94 = f32[4,1536]{1,0:T(4,128)S(1)} fusion(f32[4,512,1536]{2,1,0:T(8,128)} %get-tuple-element.194, f32[4,1536]{1,0:T(4,128)S(1)} %select_maximum_fusion.2, pred[1536,512]{0,1:T(8,128)(4,1)S(1)} %broadcast_compare_fusion.3), kind=kLoop, calls=%fused_computation.5.clone.1 | loop fusion | flops 15722496 | bytes 13418496 | tf_op jit(solution)/shard_map/while/body/eval_jaxpr/reduce_sum | solution.py:59
  156.7 1.4 copy-done.1
  158.1 6.0 %fusion.96 = f32[4,1536,64]{1,2,0:T(8,128)} fusion(f32[4,512,1536]{2,1,0:T(8,128)S(1)} %copy-done.1, f32[4,1536]{1,0:T(4,128)S(1)} %select_maximum_fusion.2, pred[1536,512]{0,1:T(8,128)(4,1)S(1)} %broadcast_compare_fusion.3, f32[4,1536,64]{1,2,0:T(8,128)} %get-tuple-element.213, f32[4,1536]{1,0:T(4,128)S(1)} %get-tuple-element.196, pred[]{:T(512)S(6)} %compare.4, ...), kind=kOutput, calls=%fused_computation.8.clone.1 | convolution fusion | flops 419561472 | bytes 16826372 | tf_op jit(solution)/shard_map/while/body/eval_jaxpr/kqj,kjd->kqd/dot_general | solution.py:60
  164.1 0.7 dynamic_slice.33
  166.6 8.1 %fusion.93 = (f32[4,1536]{1,0:T(4,128)S(1)}, f32[4,512,1536]{2,1,0:T(8,128)}) fusion(pred[1536,512]{0,1:T(8,128)(4,1)S(1)} %broadcast_compare_fusion.3, bf16[4,1536,64]{1,2,0:T(8,128)(2,1)} %get-tuple-element.229, bf16[4,2560,64]{1,2,0:T(8,128)(2,1)} %get-tuple-element.228, s32[]{:T(128)S(6)} %select_n.102), kind=kOutput, calls=%fused_computation.3.clone.1 | convolution fusion | flops 412084224 | bytes 14442500 | tf_op jit(solution)/shard_map/while/body/eval_jaxpr/kqd,kjd->kqj/dot_general | solution.py:51
  174.7 6.9 %fusion.94 = f32[4,1536]{1,0:T(4,128)S(1)} fusion(f32[4,512,1536]{2,1,0:T(8,128)} %get-tuple-element.194, f32[4,1536]{1,0:T(4,128)S(1)} %select_maximum_fusion.2, pred[1536,512]{0,1:T(8,128)(4,1)S(1)} %broadcast_compare_fusion.3), kind=kLoop, calls=%fused_computation.5.clone.1 | loop fusion | flops 15722496 | bytes 13418496 | tf_op jit(solution)/shard_map/while/body/eval_jaxpr/reduce_sum | solution.py:59
  181.6 1.4 copy-done.1
  182.9 6.0 %fusion.96 = f32[4,1536,64]{1,2,0:T(8,128)} fusion(f32[4,512,1536]{2,1,0:T(8,128)S(1)} %copy-done.1, f32[4,1536]{1,0:T(4,128)S(1)} %select_maximum_fusion.2, pred[1536,512]{0,1:T(8,128)(4,1)S(1)} %broadcast_compare_fusion.3, f32[4,1536,64]{1,2,0:T(8,128)} %get-tuple-element.213, f32[4,1536]{1,0:T(4,128)S(1)} %get-tuple-element.196, pred[]{:T(512)S(6)} %compare.4, ...), kind=kOutput, calls=%fused_computation.8.clone.1 | convolution fusion | flops 419561472 | bytes 16826372 | tf_op jit(solution)/shard_map/while/body/eval_jaxpr/kqj,kjd->kqd/dot_general | solution.py:60
  188.9 1.5 divide_convert_fusion
  190.4 1.5 copy.40
  191.9 1.8 convert_element_type.91
  194.2 2.6 convolution_convert_fusion
  198.6 1.2 reduce-window.6
  200.4 22.6 %reduce-scatter.2.cloned.1.call-done = bf16[512,768]{1,0:T(8,128)(2,1)} async-done(((bf16[512,1536]{1,0:T(8,128)(2,1)}), bf16[512,768]{1,0:T(8,128)(2,1)}) %reduce-scatter.2.cloned.1.call-update) | async-done | bytes 786448 | tf_op jit(solution)/shard_map/reduce_scatter | solution.py:136
  223.1 1.5 fusion.28
  224.5 5.2 %psum.7 = f32[512]{0:T(512)S(1)} all-reduce(f32[512]{0:T(512)S(1)} %fusion.28), channel_id=1, replica_groups=mesh['req'=16,'ep'=2] {'ep'}, use_global_device_ids=true, to_apply=%region_12.13 | all-reduce | flops 512 | bytes 4096 | tf_op jit(solution)/shard_map/psum | solution.py:145
  229.7 3.2 fusion.40
  232.9 4.6 %all-to-all-start = ((bf16[4,192,768]{2,1,0:T(8,128)(2,1)}), bf16[4,192,768]{2,1,0:T(8,128)(2,1)}, u32[]{:S(2)}, u32[]{:S(2)}) async-start(bf16[4,192,768]{2,1,0:T(8,128)(2,1)} %fusion.40), calls=%async_computation.1 | async-start | bytes 2359296 | tf_op jit(solution)/shard_map/all_to_all | solution.py:156
  238.0 14.2 %all-to-all-done = bf16[4,192,768]{2,1,0:T(8,128)(2,1)} async-done(((bf16[4,192,768]{2,1,0:T(8,128)(2,1)}), bf16[4,192,768]{2,1,0:T(8,128)(2,1)}, u32[]{:S(2)}, u32[]{:S(2)}) %all-to-all-start) | async-done | bytes 1179680 | tf_op jit(solution)/shard_map/all_to_all | solution.py:156
  252.2 2.4 copy.45
  254.6 3.9 %fusion.68 = f32[2,192,512]{2,1,0:T(8,128)} fusion(bf16[2,192,1536]{2,1,0:T(8,128)(2,1)} %bitcast.104, bf16[2,1536,512]{2,1,0:T(8,128)(2,1)} %all-gather.6.cloned.1.call-done), kind=kOutput, calls=%fused_computation.103 | convolution fusion | flops 603979776 | bytes 5111808 | tf_op jit(solution)/shard_map/ecd,edf->ecf/dot_general | solution.py:159
  258.5 32.5 %all-gather.10.cloned.1.call-done = bf16[2,512,1536]{2,1,0:T(8,128)(2,1)} async-done(((bf16[2,32,1536]{2,1,0:T(8,128)(2,1)}), bf16[2,512,1536]{2,1,0:T(8,128)(2,1)}) %all-gather.10.cloned.1.call-update) | async-done | bytes 3145744 | tf_op jit(solution)/shard_map/all_gather | solution.py:176
  291.0 46.1 %all-gather.8.cloned.1.call-done = bf16[2,1536,512]{2,1,0:T(8,128)(2,1)} async-done(((bf16[2,96,512]{2,1,0:T(8,128)(2,1)}), bf16[2,1536,512]{2,1,0:T(8,128)(2,1)}) %all-gather.8.cloned.1.call-update) | async-done | bytes 3145744 | tf_op jit(solution)/shard_map/all_gather | solution.py:168
  337.2 5.9 %fusion.27 = bf16[2,192,1536]{2,1,0:T(8,128)(2,1)} fusion(bf16[2,512,1536]{2,1,0:T(8,128)(2,1)} %all-gather.10.cloned.1.call-done, f32[2,192]{1,0:T(2,128)S(1)} %constant_dynamic-slice_fusion, bf16[2,192,1536]{2,1,0:T(8,128)(2,1)} %bitcast.105, bf16[2,1536,512]{2,1,0:T(8,128)(2,1)} %all-gather.8.cloned.1.call-done, f32[2,192,512]{2,1,0:T(8,128)} %fusion.68), kind=kOutput, calls=%fused_computation.39 | convolution fusion | flops 1210318848 | bytes 9438720 | tf_op jit(solution)/shard_map/ecf,efd->ecd/dot_general | solution.py:173
  343.1 1.3 slice_bitcast_fusion.1
  344.5 18.2 %all_to_all.23 = bf16[2,2,192,768]{3,2,1,0:T(8,128)(2,1)S(1)} all-to-all(bf16[2,2,192,768]{3,2,1,0:T(8,128)(2,1)S(1)} %pad_maximum_fusion), channel_id=1, replica_groups=mesh['req'=16,'ep'=2] {'ep'}, dimensions={0} | all-to-all | bytes 2359296 | tf_op jit(solution)/shard_map/all_to_all | solution.py:182
  362.7 1.1 bitcast_reduce_fusion
  364.0 0.9 copy-done.3
  364.9 1.2 fusion.44
  (95 shorter events, 11.0 us)
Async XLA Ops:
  8.0 186.2 %copy-start = (bf16[768,1536]{1,0:T(8,128)(2,1)S(1)}, bf16[768,1536]{1,0:T(8,128)(2,1)}, u32[]{:S(2)}) copy-start(bf16[768,1536]{1,0:T(8,128)(2,1)} %param.30) | copy-start | bytes 7077892
  8.0 33.8 %all-gather.12.cloned.1.call-start = ((), (), s32[]{:S(2)}) async-start(), calls=%async_computation.7 | async-start | bytes 2359296 | tf_op jit(solution)/shard_map/all_gather | solution.py:108
  8.1 2.6 copy-start.5
  10.7 1.2 copy-start.11
  10.7 1.8 copy-start.12
  11.8 32.0 %copy-start.10 = (f32[1536]{0:T(1024)S(1)}, f32[1536]{0:T(1024)}, u32[]{:S(2)}) copy-start(f32[1536]{0:T(1024)} %param.25) | copy-start | bytes 18436
  11.8 211.3 %reduce-scatter.2.cloned.1.call-start = ((), (), s32[]{:S(2)}) async-start(), calls=%async_computation.3 | async-start | bytes 2359296 | tf_op jit(solution)/shard_map/reduce_scatter | solution.py:136
  41.8 1.9 copy-start.4
  43.8 2.2 copy-start.9
  75.6 8.3 %copy-start.1 = (f32[4,512,1536]{2,1,0:T(8,128)S(1)}, f32[4,512,1536]{2,1,0:T(8,128)}, u32[]{:S(2)}) copy-start(f32[4,512,1536]{2,1,0:T(8,128)} %get-tuple-element.194) | copy-start | bytes 37748740 | tf_op jit(solution)/shard_map/while
  100.1 8.3 %copy-start.1 = (f32[4,512,1536]{2,1,0:T(8,128)S(1)}, f32[4,512,1536]{2,1,0:T(8,128)}, u32[]{:S(2)}) copy-start(f32[4,512,1536]{2,1,0:T(8,128)} %get-tuple-element.194) | copy-start | bytes 37748740 | tf_op jit(solution)/shard_map/while
  125.0 8.3 %copy-start.1 = (f32[4,512,1536]{2,1,0:T(8,128)S(1)}, f32[4,512,1536]{2,1,0:T(8,128)}, u32[]{:S(2)}) copy-start(f32[4,512,1536]{2,1,0:T(8,128)} %get-tuple-element.194) | copy-start | bytes 37748740 | tf_op jit(solution)/shard_map/while
  149.8 8.3 %copy-start.1 = (f32[4,512,1536]{2,1,0:T(8,128)S(1)}, f32[4,512,1536]{2,1,0:T(8,128)}, u32[]{:S(2)}) copy-start(f32[4,512,1536]{2,1,0:T(8,128)} %get-tuple-element.194) | copy-start | bytes 37748740 | tf_op jit(solution)/shard_map/while
  174.7 8.3 %copy-start.1 = (f32[4,512,1536]{2,1,0:T(8,128)S(1)}, f32[4,512,1536]{2,1,0:T(8,128)}, u32[]{:S(2)}) copy-start(f32[4,512,1536]{2,1,0:T(8,128)} %get-tuple-element.194) | copy-start | bytes 37748740 | tf_op jit(solution)/shard_map/while
  196.8 1.8 copy-start.6
  196.8 3.5 copy-start.8
  196.8 26.3 %copy-start.2 = (bf16[1,512,768]{2,1,0:T(8,128)(2,1)S(1)}, bf16[1,512,768]{2,1,0:T(8,128)(2,1)}, u32[]{:S(2)}) copy-start(bf16[1,512,768]{2,1,0:T(8,128)(2,1)} %param.18) | copy-start | bytes 2359300
  196.8 57.7 %all-gather.6.cloned.1.call-start = ((), (), s32[]{:S(2)}) async-start(), calls=%async_computation.4 | async-start | bytes 3342336 | tf_op jit(solution)/shard_map/all_gather | solution.py:162
  197.4 93.6 %all-gather.10.cloned.1.call-start = ((), (), s32[]{:S(2)}) async-start(), calls=%async_computation.6 | async-start | bytes 3342336 | tf_op jit(solution)/shard_map/all_gather | solution.py:176
  198.0 139.2 %all-gather.8.cloned.1.call-start = ((), (), s32[]{:S(2)}) async-start(), calls=%async_computation.5 | async-start | bytes 3342336 | tf_op jit(solution)/shard_map/all_gather | solution.py:168
  232.9 4.6 %copy-start.7 = (f32[1,512,8]{1,2,0:T(8,128)S(1)}, f32[1,512,8]{1,2,0:T(8,128)}, u32[]{:S(2)}) copy-start(f32[1,512,8]{1,2,0:T(8,128)} %param.24) | copy-start | bytes 49156
  232.9 19.2 %all-to-all-start = ((bf16[4,192,768]{2,1,0:T(8,128)(2,1)}), bf16[4,192,768]{2,1,0:T(8,128)(2,1)}, u32[]{:S(2)}, u32[]{:S(2)}) async-start(bf16[4,192,768]{2,1,0:T(8,128)(2,1)} %fusion.40), calls=%async_computation.1 | async-start | bytes 2359296 | tf_op jit(solution)/shard_map/all_to_all | solution.py:156
  363.7 1.1 copy-start.3
Sparse Core Ops, SparseCore 0:
  11.9 29.8 all-gather.11
  197.0 26.0 reduce-scatter.1
Sparse Core Ops, SparseCore 1:
  199.6 45.5 all-gather.5
  247.3 43.7 all-gather.9
  293.5 43.7 all-gather.7
